TPU v7x, 32 devices: a whole 2x2x4 slice. The times are simulated.
32 devices in a mesh: groups: 2 (over y), freq: 4 (over z), tile: 4 (over x, core).
Axes of the slice: x: 2, y: 2, z: 4, core: 2. Of those that a mesh axis runs over, the one named last changes fastest.
Arguments:
- traces: bfloat16 [640, 32, 16384], P('freq', 'groups', 'tile'), parts along dimension 1, may hold values from -6 to 6
- v_factors: bfloat16 [4, 2, 32, 64, 8, 256], P('freq', None, None, 'tile'), may hold values from -0.375 to 0.375
- u_factors: bfloat16 [4, 2, 32, 64, 8, 256], P('freq', None, 'tile'), may hold values from -0.25 to 0.25
- ranks: int32 [4, 32, 64], P('freq', None, 'tile'), may hold values from 1 to 8
Outputs:
- convolved: bfloat16 [640, 32, 8192], P('freq', 'groups', 'tile'), parts along dimension 1
There are 2 independent parts, one for each index of `groups`. A program takes and returns all parts, laid end to end along the dimension named above; an argument that names none is the same for every part. Nothing has to cross between parts.
All inputs are finite; a program needn't handle non-finite values.
Results may differ from a plain program's by a relative error of at most 0.0074.
Values may be sent and summed in bfloat16 or wider, within the bound.
No kernel may reach another device: no remote copies, remote signals or barrier semaphores. Data moves between devices by JAX's collectives and lax.ppermute only.
A program may use at most 192 MiB of HBM per device.

v0:
```python
import math
import jax
import jax.numpy as jnp
from jax import lax
from jax.sharding import PartitionSpec as P

NT = 640
F0 = 40
CHUNKS = 2


def twiddle(freq_ids, time_ids):
    turns = (F0 + freq_ids)[:, None] * time_ids[None, :] % NT
    angle = turns.astype(jnp.float32) * (2.0 * math.pi / NT)
    return (jnp.cos(angle).astype(jnp.bfloat16), jnp.sin(angle).astype(jnp.bfloat16))


def spread_over(weights, count):
    rows, cols = weights.shape
    kind = weights.dtype
    repeat_rows = (
        jnp.arange(rows * count, dtype=jnp.int32)[:, None] // count
        == jnp.arange(rows, dtype=jnp.int32)[None, :]
    ).astype(kind)
    repeat_cols = (
        jnp.arange(cols, dtype=jnp.int32)[:, None]
        == jnp.arange(cols * count, dtype=jnp.int32)[None, :] // count
    ).astype(kind)
    tall = jnp.dot(repeat_rows, weights, preferred_element_type=jnp.float32).astype(kind)
    wide = jnp.dot(tall, repeat_cols, preferred_element_type=jnp.float32)
    same = (
        jnp.arange(rows * count, dtype=jnp.int32)[:, None] % count
        == jnp.arange(cols * count, dtype=jnp.int32)[None, :] % count
    )
    return jnp.where(same, wide, jnp.float32(0.0)).astype(kind)


def per_device(traces, v_factors, u_factors, ranks):
    time_count = traces.shape[0]
    virtual_sources = traces.shape[1]
    source_count = traces.shape[2]
    freq_local = v_factors.shape[0]
    freq_total = freq_local * lax.axis_size("freq")
    tile_width = v_factors.shape[5]
    rank_positions = v_factors.shape[4]
    rows_all = v_factors.shape[2]
    columns = v_factors.shape[3]
    time_ids = lax.axis_index("freq") * time_count + jnp.arange(time_count, dtype=jnp.int32)
    scale_time = 1.0 / math.sqrt(NT)
    freq_ids = jnp.arange(freq_total, dtype=jnp.int32)
    cosine, sine = twiddle(freq_ids, time_ids)
    chunks = CHUNKS if virtual_sources % CHUNKS == 0 else 1
    width = virtual_sources // chunks
    forward = spread_over(jnp.stack([cosine, -sine], 1).reshape(freq_total * 2, time_count), width)
    emitter_factors = v_factors[0]
    receiver_factors = u_factors[0]
    rank_mask = (
        jnp.arange(rank_positions, dtype=jnp.int32)[None, None, :, None]
        < ranks[0][:, :, None, None]
    )

    def source_product(left_operand_factors, right_operand_factors):
        return jnp.einsum(
            "ajrs,vjs->ajrv",
            left_operand_factors,
            right_operand_factors,
            preferred_element_type=jnp.float32,
        )

    def receiver_product(left_operand_factors, right_operand_factors):
        return jnp.einsum(
            "mdlh,mdlu->umh",
            left_operand_factors,
            right_operand_factors,
            preferred_element_type=jnp.float32,
        )

    sums = []
    for part in range(chunks):
        flat_traces = traces[:, part * width : (part + 1) * width, :].reshape(
            time_count * width, source_count
        )
        partial = jnp.dot(forward, flat_traces, preferred_element_type=jnp.float32).reshape(
            freq_total, 2, width, source_count
        )
        sums.append(lax.psum_scatter(partial, "freq", scatter_dimension=0, tiled=True))
    pieces = []
    for part in range(chunks):
        summed = sums[part]
        if pieces:
            summed, pieces[-1] = lax.optimization_barrier((summed, pieces[-1]))
        spectrum = (summed * scale_time).astype(jnp.bfloat16)[0]
        spectral_tiles = spectrum.reshape(2, width, columns, tile_width)
        real_coeff = source_product(emitter_factors[0], spectral_tiles[0]) - source_product(
            emitter_factors[1], spectral_tiles[1]
        )
        imag_coeff = source_product(emitter_factors[0], spectral_tiles[1]) + source_product(
            emitter_factors[1], spectral_tiles[0]
        )
        stacked = jnp.stack([real_coeff, imag_coeff])
        coefficients = jnp.where(rank_mask[None], stacked, jnp.float32(0.0)).astype(jnp.bfloat16)
        coefficients = coefficients.reshape(2, rows_all, columns, rank_positions * width)
        arrived = lax.all_to_all(coefficients, "tile", split_axis=1, concat_axis=2, tiled=True)
        rows_local = arrived.shape[1]
        columns_all = arrived.shape[2]
        arrived = arrived.reshape(2, rows_local, columns_all, rank_positions, width)
        real_recv = receiver_product(receiver_factors[0], arrived[0]) - receiver_product(
            receiver_factors[1], arrived[1]
        )
        imag_recv = receiver_product(receiver_factors[0], arrived[1]) + receiver_product(
            receiver_factors[1], arrived[0]
        )
        receivers = rows_local * tile_width
        received = (
            jnp.stack([real_recv, imag_recv]).reshape(1, 2, width, receivers).astype(jnp.bfloat16)
        )
        pieces.append(lax.all_gather(received, "freq", axis=0, tiled=True))
    piece = jnp.concatenate(pieces, axis=2)
    count = piece.shape[0]
    backward = jnp.stack([cosine.T, -sine.T], 2).reshape(time_count, count * 2)
    added = jnp.dot(
        spread_over(backward, virtual_sources),
        piece.reshape(count * 2 * virtual_sources, receivers),
        preferred_element_type=jnp.float32,
    )
    scale_freq = 1.0 / math.sqrt(freq_total)
    return (added * scale_freq).astype(jnp.bfloat16).reshape(time_count, virtual_sources, receivers)


def solution(mesh):
    placed = (
        P("freq", "groups", "tile"),
        P("freq", None, None, "tile", None, None),
        P("freq", None, "tile", None, None, None),
        P("freq", None, "tile"),
    )
    return jax.shard_map(
        per_device,
        mesh=mesh,
        in_specs=placed,
        out_specs=P("freq", "groups", "tile"),
        check_vma=False,
    )
```

profile of v0, /device:TPU:0, one launch (start us, length us, event | category | flops | bytes accessed | tf_op | source)
XLA Modules:
  0.0 136.0 jit_solution(8641000433981534925)
XLA Ops:
  6.9 0.4 fusion.7
  7.3 6.9 %fusion = f32[4,2,8,4096]{3,2,1,0:T(8,128)} fusion(bf16[4,2,8,1280]{3,2,1,0:T(8,128)(2,1)S(1)} %bitcast.242, bf16[160,16,4096]{2,1,0:T(8,128)(2,1)} %param.4), kind=kOutput, calls=%fused_computation.1 | convolution fusion | flops 671088640 | bytes 11698176 | tf_op jit(solution)/shard_map/dot_general | solution.py:83
  14.3 6.9 %fusion.2 = f32[4,2,8,4096]{3,2,1,0:T(8,128)} fusion(bf16[4,2,8,1280]{3,2,1,0:T(8,128)(2,1)S(1)} %bitcast.243, bf16[160,16,4096]{2,1,0:T(8,128)(2,1)} %param.4), kind=kOutput, calls=%fused_computation.3 | convolution fusion | flops 671088640 | bytes 11698176 | tf_op jit(solution)/shard_map/dot_general | solution.py:83
  21.6 0.2 copy.70
  21.9 5.1 %fusion.83 = (bf16[1,1,32,16,8,256]{5,4,3,2,1,0:T(8,128)(2,1)}, bf16[1,1,32,16,8,256]{5,4,3,2,1,0:T(8,128)(2,1)}) fusion(bf16[1,2,32,16,8,256]{5,4,3,2,1,0:T(8,128)(2,1)} %param.5), kind=kLoop, calls=%fused_computation.135 | loop fusion | bytes 8388608 | tf_op jit(solution)/shard_map/slice | solution.py:95
  27.0 1.7 %fusion.82 = (bf16[1,1,8,64,8,256]{5,4,3,2,1,0:T(8,128)(2,1)S(1)}, bf16[1,1,8,64,8,256]{5,4,3,2,1,0:T(8,128)(2,1)}) fusion(bf16[1,2,8,64,8,256]{5,4,3,2,1,0:T(8,128)(2,1)S(1)} %copy-done.5), kind=kLoop, calls=%fused_computation.134 | loop fusion | bytes 8388608 | tf_op jit(solution)/shard_map/slice | solution.py:107
  28.6 1.4 %convolution_convert_fusion = bf16[2560,8]{0,1:T(8,128)(2,1)S(1)} fusion(bf16[160,8]{0,1:T(8,128)(2,1)S(1)} %reshape.600, s32[2560]{0:T(1024)S(1)} %add_select_fusion), kind=kOutput, calls=%fused_computation.9 | convolution fusion | flops 6983680 | bytes 53760 | tf_op jit(solution)/shard_map/dot_general | solution.py:29
  30.0 14.2 %reduce-scatter.5.cloned.1.call-done = f32[1,2,8,4096]{3,2,1,0:T(8,128)} async-done(((f32[4,2,8,4096]{3,2,1,0:T(8,128)}), f32[1,2,8,4096]{3,2,1,0:T(8,128)}) %reduce-scatter.5.cloned.1.call-update) | async-done | bytes 262160 | tf_op jit(solution)/shard_map/reduce_scatter | solution.py:86
  44.2 1.1 multiply_convert_fusion.2
  45.4 3.2 %fusion.10 = f32[16,8,32,8]{2,1,3,0:T(8,128)S(1)} fusion(bf16[8,16,256,1]{2,0,3,1:T(8,128)(2,1)S(1)} %bitcast.229, bf16[1,1,32,16,8,256]{5,4,3,2,1,0:T(8,128)(2,1)} %get-tuple-element.12), kind=kOutput, calls=%fused_computation.19 | convolution fusion | flops 16777216 | bytes 2293760 | tf_op jit(solution)/shard_map/ajrs,vjs->ajrv/dot_general | solution.py:63
  48.6 1.5 %fusion.11 = f32[16,8,32,8]{2,1,3,0:T(8,128)S(1)} fusion(bf16[8,16,256,1]{2,0,3,1:T(8,128)(2,1)S(1)} %bitcast.233, bf16[1,1,32,16,8,256]{5,4,3,2,1,0:T(8,128)(2,1)S(1)} %copy-done.3), kind=kOutput, calls=%fused_computation.20 | convolution fusion | flops 16777216 | bytes 2293760 | tf_op jit(solution)/shard_map/ajrs,vjs->ajrv/dot_general | solution.py:63
  50.1 1.5 %fusion.28 = bf16[1,32,16,64]{1,3,2,0:T(8,128)(2,1)S(1)} fusion(f32[16,8,32,8]{2,1,3,0:T(8,128)S(1)} %fusion.10, bf16[8,16,256,1]{2,0,3,1:T(8,128)(2,1)S(1)} %bitcast.234, bf16[1,1,32,16,8,256]{5,4,3,2,1,0:T(8,128)(2,1)S(1)} %copy-done.1), kind=kOutput, calls=%fused_computation.37 | convolution fusion | flops 16842752 | bytes 2359296 | tf_op jit(solution)/shard_map/ajrs,vjs->ajrv/dot_general | solution.py:63
  51.6 0.2 copy.74
  51.8 3.1 %fusion.26 = bf16[1,32,16,64]{1,3,2,0:T(8,128)(2,1)S(1)} fusion(f32[16,8,32,8]{2,1,3,0:T(8,128)S(1)} %fusion.11, bf16[8,16,256,1]{2,0,3,1:T(8,128)(2,1)S(1)} %bitcast.230, bf16[1,1,32,16,8,256]{5,4,3,2,1,0:T(8,128)(2,1)} %get-tuple-element.11), kind=kOutput, calls=%fused_computation.35 | convolution fusion | flops 16842752 | bytes 2359296 | tf_op jit(solution)/shard_map/ajrs,vjs->ajrv/dot_general | solution.py:63
  54.9 0.2 copy.73
  55.2 0.9 reshape.620
  56.1 3.5 %all-to-all-start = ((bf16[4,2,8192]{2,1,0:T(2,128)(2,1)}), bf16[4,2,8192]{2,1,0:T(2,128)(2,1)S(1)}, u32[]{:S(2)}, u32[]{:S(2)}) async-start(bf16[4,2,8192]{2,1,0:T(2,128)(2,1)} %reshape.620), calls=%async_computation.2 | async-start | bytes 262144 | tf_op jit(solution)/shard_map/all_to_all | solution.py:103
  59.6 4.4 %all-to-all-done = bf16[4,2,8192]{2,1,0:T(2,128)(2,1)S(1)} async-done(((bf16[4,2,8192]{2,1,0:T(2,128)(2,1)}), bf16[4,2,8192]{2,1,0:T(2,128)(2,1)S(1)}, u32[]{:S(2)}, u32[]{:S(2)}) %all-to-all-start) | async-done | bytes 131104 | tf_op jit(solution)/shard_map/all_to_all | solution.py:103
  64.0 0.2 reshape.621
  64.3 0.3 copy.78
  64.6 0.3 squeeze.30
  64.9 0.3 copy.76
  65.2 0.3 squeeze.28
  65.5 2.2 %fusion.34 = f32[8,8,256]{2,1,0:T(8,128)S(1)} fusion(bf16[8,64,8,8]{1,3,2,0:T(8,128)(2,1)S(1)} %squeeze.28, bf16[1,1,8,64,8,256]{5,4,3,2,1,0:T(8,128)(2,1)} %get-tuple-element.10), kind=kOutput, calls=%fused_computation.43 | convolution fusion | flops 16777216 | bytes 2228224 | tf_op jit(solution)/shard_map/mdlh,mdlu->umh/dot_general | solution.py:71
  67.8 0.5 fusion.33
  68.3 0.5 fusion.46
  68.8 0.5 fusion.45
  69.3 14.4 %all_gather.6 = bf16[4,2,8,2048]{3,2,1,0:T(8,128)(2,1)S(1)} all-gather(bf16[1,2,8,2048]{3,2,1,0:T(8,128)(2,1)S(1)} %pad_maximum_fusion.1), channel_id=1, replica_groups=mesh['groups'=2,'freq'=4,'tile'=4] {'freq'}, dimensions={0}, use_global_device_ids=true | all-gather | bytes 327680 | tf_op jit(solution)/shard_map/all_gather | solution.py:117
  83.8 1.1 multiply_convert_fusion.1
  84.9 3.2 %fusion.8 = f32[16,8,32,8]{2,1,3,0:T(8,128)S(1)} fusion(bf16[8,16,256,1]{2,0,3,1:T(8,128)(2,1)S(1)} %bitcast.231, bf16[1,1,32,16,8,256]{5,4,3,2,1,0:T(8,128)(2,1)} %get-tuple-element.12), kind=kOutput, calls=%fused_computation.17 | convolution fusion | flops 16777216 | bytes 2293760 | tf_op jit(solution)/shard_map/ajrs,vjs->ajrv/dot_general | solution.py:63
  88.1 1.5 %fusion.9 = f32[16,8,32,8]{2,1,3,0:T(8,128)S(1)} fusion(bf16[8,16,256,1]{2,0,3,1:T(8,128)(2,1)S(1)} %bitcast.235, bf16[1,1,32,16,8,256]{5,4,3,2,1,0:T(8,128)(2,1)S(1)} %copy-done.4), kind=kOutput, calls=%fused_computation.18 | convolution fusion | flops 16777216 | bytes 2293760 | tf_op jit(solution)/shard_map/ajrs,vjs->ajrv/dot_general | solution.py:63
  89.6 1.5 %fusion.32 = bf16[1,32,16,64]{1,3,2,0:T(8,128)(2,1)S(1)} fusion(f32[16,8,32,8]{2,1,3,0:T(8,128)S(1)} %fusion.8, bf16[8,16,256,1]{2,0,3,1:T(8,128)(2,1)S(1)} %bitcast.236, bf16[1,1,32,16,8,256]{5,4,3,2,1,0:T(8,128)(2,1)S(1)} %copy-done.2), kind=kOutput, calls=%fused_computation.41 | convolution fusion | flops 16842752 | bytes 2359296 | tf_op jit(solution)/shard_map/ajrs,vjs->ajrv/dot_general | solution.py:63
  91.2 1.5 %fusion.30 = bf16[1,32,16,64]{1,3,2,0:T(8,128)(2,1)S(1)} fusion(f32[16,8,32,8]{2,1,3,0:T(8,128)S(1)} %fusion.9, bf16[8,16,256,1]{2,0,3,1:T(8,128)(2,1)S(1)} %bitcast.232, bf16[1,1,32,16,8,256]{5,4,3,2,1,0:T(8,128)(2,1)S(1)} %copy-done.2), kind=kOutput, calls=%fused_computation.39 | convolution fusion | flops 16842752 | bytes 2359296 | tf_op jit(solution)/shard_map/ajrs,vjs->ajrv/dot_general | solution.py:63
  92.7 0.2 copy.80
  93.1 0.9 reshape.622
  94.0 3.5 %all-to-all-start.1 = ((bf16[4,2,8192]{2,1,0:T(2,128)(2,1)}), bf16[4,2,8192]{2,1,0:T(2,128)(2,1)S(1)}, u32[]{:S(2)}, u32[]{:S(2)}) async-start(bf16[4,2,8192]{2,1,0:T(2,128)(2,1)} %reshape.622), calls=%async_computation.3 | async-start | bytes 262144 | tf_op jit(solution)/shard_map/all_to_all | solution.py:103
  97.6 4.4 %all-to-all-done.1 = bf16[4,2,8192]{2,1,0:T(2,128)(2,1)S(1)} async-done(((bf16[4,2,8192]{2,1,0:T(2,128)(2,1)}), bf16[4,2,8192]{2,1,0:T(2,128)(2,1)S(1)}, u32[]{:S(2)}, u32[]{:S(2)}) %all-to-all-start.1) | async-done | bytes 131104 | tf_op jit(solution)/shard_map/all_to_all | solution.py:103
  102.0 0.2 reshape.623
  102.2 0.3 copy.84
  102.6 0.3 squeeze.69
  102.8 2.1 %fusion.35 = f32[8,8,256]{2,1,0:T(8,128)S(1)} fusion(bf16[8,64,8,8]{1,3,2,0:T(8,128)(2,1)S(1)} %squeeze.69, bf16[1,1,8,64,8,256]{5,4,3,2,1,0:T(8,128)(2,1)} %get-tuple-element.10), kind=kOutput, calls=%fused_computation.44 | convolution fusion | flops 16777216 | bytes 2228224 | tf_op jit(solution)/shard_map/mdlh,mdlu->umh/dot_general | solution.py:71
  104.9 0.3 copy.83
  105.3 0.3 squeeze.68
  105.6 2.1 %fusion.36 = f32[8,8,256]{2,1,0:T(8,128)S(1)} fusion(bf16[8,64,8,8]{1,3,2,0:T(8,128)(2,1)S(1)} %squeeze.68, bf16[1,1,8,64,8,256]{5,4,3,2,1,0:T(8,128)(2,1)} %get-tuple-element.10), kind=kOutput, calls=%fused_computation.45 | convolution fusion | flops 16777216 | bytes 2228224 | tf_op jit(solution)/shard_map/mdlh,mdlu->umh/dot_general | solution.py:71
  107.7 0.5 fusion.47
  108.2 0.5 fusion.48
  108.7 14.4 %all_gather.7 = bf16[4,2,8,2048]{3,2,1,0:T(8,128)(2,1)S(1)} all-gather(bf16[1,2,8,2048]{3,2,1,0:T(8,128)(2,1)S(1)} %pad_maximum_fusion.2), channel_id=1, replica_groups=mesh['groups'=2,'freq'=4,'tile'=4] {'freq'}, dimensions={0}, use_global_device_ids=true | all-gather | bytes 327680 | tf_op jit(solution)/shard_map/all_gather | solution.py:117
  123.1 6.0 %multiply_convert_fusion = bf16[2560,2048]{1,0:T(8,128)(2,1)} fusion(bf16[128,2048]{1,0:T(8,128)(2,1)S(1)} %bitcast.224, bf16[2560,8]{0,1:T(8,128)(2,1)S(1)} %convolution_convert_fusion, s32[128]{0:T(128)S(1)} %get-tuple-element.26, s32[2560]{0:T(1024)S(1)} %add_select_fusion.1, s32[128]{0:T(128)S(1)} %get-tuple-element.25), kind=kOutput, calls=%fused_computation | convolution fusion | flops 1358889984 | bytes 11062272 | tf_op jit(solution)/shard_map/dot_general | solution.py:121
  (50 shorter events, 1.4 us)
Async XLA Ops:
  6.5 37.7 %reduce-scatter.5.cloned.1.call-start = ((), (), s32[]{:S(2)}) async-start(), calls=%async_computation.5 | async-start | bytes 1310720 | tf_op jit(solution)/shard_map/reduce_scatter | solution.py:86
  14.2 7.3 %copy-start.6 = (s32[1,32,16]{1,2,0:T(8,128)S(1)}, s32[1,32,16]{1,2,0:T(8,128)}, u32[]{:S(2)}) copy-start(s32[1,32,16]{1,2,0:T(8,128)} %param.7) | copy-start | bytes 6148
  14.2 69.5 %reduce-scatter.3.cloned.1.call-start = ((), (), s32[]{:S(2)}) async-start(), calls=%async_computation.4 | async-start | bytes 1310720 | tf_op jit(solution)/shard_map/reduce_scatter | solution.py:86
  21.9 5.1 %copy-start.5 = (bf16[1,2,8,64,8,256]{5,4,3,2,1,0:T(8,128)(2,1)S(1)}, bf16[1,2,8,64,8,256]{5,4,3,2,1,0:T(8,128)(2,1)}, u32[]{:S(2)}) copy-start(bf16[1,2,8,64,8,256]{5,4,3,2,1,0:T(8,128)(2,1)} %param.6) | copy-start | bytes 12582916
  44.2 4.4 %copy-start.3 = (bf16[1,1,32,16,8,256]{5,4,3,2,1,0:T(8,128)(2,1)S(1)}, bf16[1,1,32,16,8,256]{5,4,3,2,1,0:T(8,128)(2,1)}, u32[]{:S(2)}) copy-start(bf16[1,1,32,16,8,256]{5,4,3,2,1,0:T(8,128)(2,1)} %get-tuple-element.12) | copy-start | bytes 6291460
  45.3 4.7 %copy-start.1 = (bf16[1,1,32,16,8,256]{5,4,3,2,1,0:T(8,128)(2,1)S(1)}, bf16[1,1,32,16,8,256]{5,4,3,2,1,0:T(8,128)(2,1)}, u32[]{:S(2)}) copy-start(bf16[1,1,32,16,8,256]{5,4,3,2,1,0:T(8,128)(2,1)} %get-tuple-element.11) | copy-start | bytes 6291460
  56.1 7.9 %all-to-all-start = ((bf16[4,2,8192]{2,1,0:T(2,128)(2,1)}), bf16[4,2,8192]{2,1,0:T(2,128)(2,1)S(1)}, u32[]{:S(2)}, u32[]{:S(2)}) async-start(bf16[4,2,8192]{2,1,0:T(2,128)(2,1)} %reshape.620), calls=%async_computation.2 | async-start | bytes 262144 | tf_op jit(solution)/shard_map/all_to_all | solution.py:103
  65.5 2.3 %copy-start = (bf16[1,1,8,64,8,256]{5,4,3,2,1,0:T(8,128)(2,1)S(1)}, bf16[1,1,8,64,8,256]{5,4,3,2,1,0:T(8,128)(2,1)}, u32[]{:S(2)}) copy-start(bf16[1,1,8,64,8,256]{5,4,3,2,1,0:T(8,128)(2,1)} %get-tuple-element.10) | copy-start | bytes 6291460
  83.8 4.4 %copy-start.4 = (bf16[1,1,32,16,8,256]{5,4,3,2,1,0:T(8,128)(2,1)S(1)}, bf16[1,1,32,16,8,256]{5,4,3,2,1,0:T(8,128)(2,1)}, u32[]{:S(2)}) copy-start(bf16[1,1,32,16,8,256]{5,4,3,2,1,0:T(8,128)(2,1)} %get-tuple-element.12) | copy-start | bytes 6291460
  84.9 4.7 %copy-start.2 = (bf16[1,1,32,16,8,256]{5,4,3,2,1,0:T(8,128)(2,1)S(1)}, bf16[1,1,32,16,8,256]{5,4,3,2,1,0:T(8,128)(2,1)}, u32[]{:S(2)}) copy-start(bf16[1,1,32,16,8,256]{5,4,3,2,1,0:T(8,128)(2,1)} %get-tuple-element.11) | copy-start | bytes 6291460
  94.0 7.9 %all-to-all-start.1 = ((bf16[4,2,8192]{2,1,0:T(2,128)(2,1)}), bf16[4,2,8192]{2,1,0:T(2,128)(2,1)S(1)}, u32[]{:S(2)}, u32[]{:S(2)}) async-start(bf16[4,2,8192]{2,1,0:T(2,128)(2,1)} %reshape.622), calls=%async_computation.3 | async-start | bytes 262144 | tf_op jit(solution)/shard_map/all_to_all | solution.py:103
Sparse Core Ops, SparseCore 0:
  14.3 29.8 reduce-scatter.4
  46.6 25.7 reduce-scatter.2
where the time goes:
time: 137 us; the launch traced here: 136 us
  matrix products  47.6 us (35%)
  blocking collectives  28.8 us (21%)
  waiting for transfers between devices  23 us (17%)
  between operations  13.8 us (10%)
  local copies, waits for them, and re-layouts  12.6 us (9%)
  starting transfers between devices  7.09 us (5%)
  other arithmetic  3.11 us (2%)
    all_gather x2, blocking collectives, per_device(): pieces.append(lax.all_gather(received, 'freq', axis=0, tiled=True))  28.8 us
    dot_general x8, matrix products, source_product(): jnp.einsum('ajrs,vjs->ajrv', left_operand_factors, right_operand_factors,...  17.1 us
    reduce_scatter x2, waiting for transfers between devices, per_device(): lax.psum_scatter(partial, 'freq', scatter_dimension=0, tiled=True)  14.2 us
    dot_general x2, matrix products, per_device(): jnp.dot(forward, flat_traces, preferred_element_type=jnp.float32)  13.8 us
    dot_general x8, matrix products, receiver_product(): jnp.einsum('mdlh,mdlu->umh', left_operand_factors, right_operand_factors,...  8.98 us
    all_to_all x2, waiting for transfers between devices, per_device(): lax.all_to_all(coefficients, 'tile', split_axis=1, concat_axis=2, tiled=T...  8.77 us
    all_to_all x2, starting transfers between devices, per_device(): lax.all_to_all(coefficients, 'tile', split_axis=1, concat_axis=2, tiled=T...  7.05 us
    dot_general x1, matrix products, per_device(): jnp.dot(spread_over(backward, virtual_sources), piece.reshape(count * 2 *...  6.02 us
  transfers between devices with their start and end apart: 4, of which 3 were waited for; matrix products, arithmetic and copies ran while one was open for 24% of the time, Pallas kernels for 0%

commit v1 on v0

--- a/solution.py
+++ b/solution.py
@@ -100,7 +100,12 @@
         stacked = jnp.stack([real_coeff, imag_coeff])
         coefficients = jnp.where(rank_mask[None], stacked, jnp.float32(0.0)).astype(jnp.bfloat16)
         coefficients = coefficients.reshape(2, rows_all, columns, rank_positions * width)
-        arrived = lax.all_to_all(coefficients, "tile", split_axis=1, concat_axis=2, tiled=True)
+        arrived = jnp.concatenate(
+            lax.all_to_all(
+                jnp.stack(jnp.split(coefficients, lax.axis_size("tile"), axis=1)), "tile", 0, 0
+            ),
+            axis=2,
+        )
         rows_local = arrived.shape[1]
         columns_all = arrived.shape[2]
         arrived = arrived.reshape(2, rows_local, columns_all, rank_positions, width)

time: 137 us -> 137 us (level)
  no operation moved by 1% of the time
where the time goes in v1:
time: 137 us; the launch traced here: 136 us
  matrix products  47.6 us (35%)
  blocking collectives  28.8 us (21%)
  waiting for transfers between devices  23 us (17%)
  between operations  13.8 us (10%)
  local copies, waits for them, and re-layouts  12.5 us (9%)
  starting transfers between devices  7.09 us (5%)
  other arithmetic  3.22 us (2%)
    all_gather x2, blocking collectives, per_device(): pieces.append(lax.all_gather(received, 'freq', axis=0, tiled=True))  28.8 us
    dot_general x8, matrix products, source_product(): jnp.einsum('ajrs,vjs->ajrv', left_operand_factors, right_operand_factors,...  17.1 us
    reduce_scatter x2, waiting for transfers between devices, per_device(): lax.psum_scatter(partial, 'freq', scatter_dimension=0, tiled=True)  14.2 us
    dot_general x2, matrix products, per_device(): jnp.dot(forward, flat_traces, preferred_element_type=jnp.float32)  13.8 us
    dot_general x8, matrix products, receiver_product(): jnp.einsum('mdlh,mdlu->umh', left_operand_factors, right_operand_factors,...  8.98 us
    all_to_all x2, waiting for transfers between devices, per_device(): lax.all_to_all(jnp.stack(jnp.split(coefficients, lax.axis_size('tile'), a...  8.77 us
    all_to_all x2, starting transfers between devices, per_device(): lax.all_to_all(jnp.stack(jnp.split(coefficients, lax.axis_size('tile'), a...  7.05 us
    dot_general x1, matrix products, per_device(): jnp.dot(spread_over(backward, virtual_sources), piece.reshape(count * 2 *...  6.02 us
  transfers between devices with their start and end apart: 4, of which 3 were waited for; matrix products, arithmetic and copies ran while one was open for 24% of the time, Pallas kernels for 0%

profile of v1, /device:TPU:0, one launch (start us, length us, event | category | flops | bytes accessed | tf_op | source)
XLA Modules:
  0.0 136.1 jit_solution(8615095730629220018)
XLA Ops:
  6.9 0.4 fusion.7
  7.3 6.9 %fusion = f32[4,2,8,4096]{3,2,1,0:T(8,128)} fusion(bf16[4,2,8,1280]{3,2,1,0:T(8,128)(2,1)S(1)} %bitcast.246, bf16[160,16,4096]{2,1,0:T(8,128)(2,1)} %param.4), kind=kOutput, calls=%fused_computation.1 | convolution fusion | flops 671088640 | bytes 11698176 | tf_op jit(solution)/shard_map/dot_general | solution.py:83
  14.3 6.9 %fusion.2 = f32[4,2,8,4096]{3,2,1,0:T(8,128)} fusion(bf16[4,2,8,1280]{3,2,1,0:T(8,128)(2,1)S(1)} %bitcast.247, bf16[160,16,4096]{2,1,0:T(8,128)(2,1)} %param.4), kind=kOutput, calls=%fused_computation.3 | convolution fusion | flops 671088640 | bytes 11698176 | tf_op jit(solution)/shard_map/dot_general | solution.py:83
  21.6 0.2 copy.82
  21.9 5.1 %fusion.83 = (bf16[1,1,32,16,8,256]{5,4,3,2,1,0:T(8,128)(2,1)}, bf16[1,1,32,16,8,256]{5,4,3,2,1,0:T(8,128)(2,1)}) fusion(bf16[1,2,32,16,8,256]{5,4,3,2,1,0:T(8,128)(2,1)} %param.5), kind=kLoop, calls=%fused_computation.145 | loop fusion | bytes 8388608 | tf_op jit(solution)/shard_map/slice | solution.py:95
  27.0 1.6 %fusion.82 = (bf16[1,1,8,64,8,256]{5,4,3,2,1,0:T(8,128)(2,1)S(1)}, bf16[1,1,8,64,8,256]{5,4,3,2,1,0:T(8,128)(2,1)}) fusion(bf16[1,2,8,64,8,256]{5,4,3,2,1,0:T(8,128)(2,1)S(1)} %copy-done.5), kind=kLoop, calls=%fused_computation.144 | loop fusion | bytes 8388608 | tf_op jit(solution)/shard_map/slice | solution.py:112
  28.6 1.4 %convolution_convert_fusion = bf16[2560,8]{0,1:T(8,128)(2,1)S(1)} fusion(bf16[160,8]{0,1:T(8,128)(2,1)S(1)} %reshape.602, s32[2560]{0:T(1024)S(1)} %add_select_fusion), kind=kOutput, calls=%fused_computation.9 | convolution fusion | flops 6983680 | bytes 53760 | tf_op jit(solution)/shard_map/dot_general | solution.py:29
  30.0 14.2 %reduce-scatter.5.cloned.1.call-done = f32[1,2,8,4096]{3,2,1,0:T(8,128)} async-done(((f32[4,2,8,4096]{3,2,1,0:T(8,128)}), f32[1,2,8,4096]{3,2,1,0:T(8,128)}) %reduce-scatter.5.cloned.1.call-update) | async-done | bytes 262160 | tf_op jit(solution)/shard_map/reduce_scatter | solution.py:86
  44.2 1.1 multiply_convert_fusion.2
  45.3 3.2 %fusion.10 = f32[16,8,32,8]{2,1,3,0:T(8,128)S(1)} fusion(bf16[8,16,256,1]{2,0,3,1:T(8,128)(2,1)S(1)} %bitcast.233, bf16[1,1,32,16,8,256]{5,4,3,2,1,0:T(8,128)(2,1)} %get-tuple-element.12), kind=kOutput, calls=%fused_computation.19 | convolution fusion | flops 16777216 | bytes 2293760 | tf_op jit(solution)/shard_map/ajrs,vjs->ajrv/dot_general | solution.py:63
  48.6 1.5 %fusion.11 = f32[16,8,32,8]{2,1,3,0:T(8,128)S(1)} fusion(bf16[8,16,256,1]{2,0,3,1:T(8,128)(2,1)S(1)} %bitcast.237, bf16[1,1,32,16,8,256]{5,4,3,2,1,0:T(8,128)(2,1)S(1)} %copy-done.3), kind=kOutput, calls=%fused_computation.20 | convolution fusion | flops 16777216 | bytes 2293760 | tf_op jit(solution)/shard_map/ajrs,vjs->ajrv/dot_general | solution.py:63
  50.1 1.5 %fusion.28 = bf16[1,32,16,64]{1,3,2,0:T(8,128)(2,1)S(1)} fusion(f32[16,8,32,8]{2,1,3,0:T(8,128)S(1)} %fusion.10, bf16[8,16,256,1]{2,0,3,1:T(8,128)(2,1)S(1)} %bitcast.238, bf16[1,1,32,16,8,256]{5,4,3,2,1,0:T(8,128)(2,1)S(1)} %copy-done.1), kind=kOutput, calls=%fused_computation.37 | convolution fusion | flops 16842752 | bytes 2359296 | tf_op jit(solution)/shard_map/ajrs,vjs->ajrv/dot_general | solution.py:63
  51.6 0.2 copy.86
  51.8 3.1 %fusion.26 = bf16[1,32,16,64]{1,3,2,0:T(8,128)(2,1)S(1)} fusion(f32[16,8,32,8]{2,1,3,0:T(8,128)S(1)} %fusion.11, bf16[8,16,256,1]{2,0,3,1:T(8,128)(2,1)S(1)} %bitcast.234, bf16[1,1,32,16,8,256]{5,4,3,2,1,0:T(8,128)(2,1)} %get-tuple-element.11), kind=kOutput, calls=%fused_computation.35 | convolution fusion | flops 16842752 | bytes 2359296 | tf_op jit(solution)/shard_map/ajrs,vjs->ajrv/dot_general | solution.py:63
  54.9 0.2 copy.85
  55.3 0.9 reshape.624
  56.2 3.5 %all-to-all-start = ((bf16[4,2,8192]{2,1,0:T(2,128)(2,1)}), bf16[4,2,8192]{2,1,0:T(2,128)(2,1)S(1)}, u32[]{:S(2)}, u32[]{:S(2)}) async-start(bf16[4,2,8192]{2,1,0:T(2,128)(2,1)} %reshape.624), calls=%async_computation.2 | async-start | bytes 262144 | tf_op jit(solution)/shard_map/all_to_all | solution.py:104
  59.7 4.4 %all-to-all-done = bf16[4,2,8192]{2,1,0:T(2,128)(2,1)S(1)} async-done(((bf16[4,2,8192]{2,1,0:T(2,128)(2,1)}), bf16[4,2,8192]{2,1,0:T(2,128)(2,1)S(1)}, u32[]{:S(2)}, u32[]{:S(2)}) %all-to-all-start) | async-done | bytes 131104 | tf_op jit(solution)/shard_map/all_to_all | solution.py:104
  64.1 0.2 reshape.625
  64.4 0.3 copy.89
  64.7 0.3 squeeze.30
  65.0 0.3 copy.87
  65.3 0.3 squeeze.28
  65.6 2.2 %fusion.34 = f32[8,8,256]{2,1,0:T(8,128)S(1)} fusion(bf16[8,64,8,8]{1,3,2,0:T(8,128)(2,1)S(1)} %squeeze.28, bf16[1,1,8,64,8,256]{5,4,3,2,1,0:T(8,128)(2,1)} %get-tuple-element.10), kind=kOutput, calls=%fused_computation.43 | convolution fusion | flops 16777216 | bytes 2228224 | tf_op jit(solution)/shard_map/mdlh,mdlu->umh/dot_general | solution.py:71
  67.8 0.5 fusion.33
  68.3 0.5 fusion.46
  68.8 0.5 fusion.45
  69.4 14.4 %all_gather.6 = bf16[4,2,8,2048]{3,2,1,0:T(8,128)(2,1)S(1)} all-gather(bf16[1,2,8,2048]{3,2,1,0:T(8,128)(2,1)S(1)} %pad_maximum_fusion.3), channel_id=1, replica_groups=mesh['groups'=2,'freq'=4,'tile'=4] {'freq'}, dimensions={0}, use_global_device_ids=true | all-gather | bytes 327680 | tf_op jit(solution)/shard_map/all_gather | solution.py:122
  83.8 1.1 multiply_convert_fusion.1
  85.0 3.2 %fusion.8 = f32[16,8,32,8]{2,1,3,0:T(8,128)S(1)} fusion(bf16[8,16,256,1]{2,0,3,1:T(8,128)(2,1)S(1)} %bitcast.235, bf16[1,1,32,16,8,256]{5,4,3,2,1,0:T(8,128)(2,1)} %get-tuple-element.12), kind=kOutput, calls=%fused_computation.17 | convolution fusion | flops 16777216 | bytes 2293760 | tf_op jit(solution)/shard_map/ajrs,vjs->ajrv/dot_general | solution.py:63
  88.2 1.5 %fusion.9 = f32[16,8,32,8]{2,1,3,0:T(8,128)S(1)} fusion(bf16[8,16,256,1]{2,0,3,1:T(8,128)(2,1)S(1)} %bitcast.239, bf16[1,1,32,16,8,256]{5,4,3,2,1,0:T(8,128)(2,1)S(1)} %copy-done.4), kind=kOutput, calls=%fused_computation.18 | convolution fusion | flops 16777216 | bytes 2293760 | tf_op jit(solution)/shard_map/ajrs,vjs->ajrv/dot_general | solution.py:63
  89.7 1.5 %fusion.32 = bf16[1,32,16,64]{1,3,2,0:T(8,128)(2,1)S(1)} fusion(f32[16,8,32,8]{2,1,3,0:T(8,128)S(1)} %fusion.8, bf16[8,16,256,1]{2,0,3,1:T(8,128)(2,1)S(1)} %bitcast.240, bf16[1,1,32,16,8,256]{5,4,3,2,1,0:T(8,128)(2,1)S(1)} %copy-done.2), kind=kOutput, calls=%fused_computation.41 | convolution fusion | flops 16842752 | bytes 2359296 | tf_op jit(solution)/shard_map/ajrs,vjs->ajrv/dot_general | solution.py:63
  91.2 1.5 %fusion.30 = bf16[1,32,16,64]{1,3,2,0:T(8,128)(2,1)S(1)} fusion(f32[16,8,32,8]{2,1,3,0:T(8,128)S(1)} %fusion.9, bf16[8,16,256,1]{2,0,3,1:T(8,128)(2,1)S(1)} %bitcast.236, bf16[1,1,32,16,8,256]{5,4,3,2,1,0:T(8,128)(2,1)S(1)} %copy-done.2), kind=kOutput, calls=%fused_computation.39 | convolution fusion | flops 16842752 | bytes 2359296 | tf_op jit(solution)/shard_map/ajrs,vjs->ajrv/dot_general | solution.py:63
  92.7 0.2 copy.91
  93.3 0.9 reshape.626
  94.2 3.5 %all-to-all-start.1 = ((bf16[4,2,8192]{2,1,0:T(2,128)(2,1)}), bf16[4,2,8192]{2,1,0:T(2,128)(2,1)S(1)}, u32[]{:S(2)}, u32[]{:S(2)}) async-start(bf16[4,2,8192]{2,1,0:T(2,128)(2,1)} %reshape.626), calls=%async_computation.3 | async-start | bytes 262144 | tf_op jit(solution)/shard_map/all_to_all | solution.py:104
  97.8 4.4 %all-to-all-done.1 = bf16[4,2,8192]{2,1,0:T(2,128)(2,1)S(1)} async-done(((bf16[4,2,8192]{2,1,0:T(2,128)(2,1)}), bf16[4,2,8192]{2,1,0:T(2,128)(2,1)S(1)}, u32[]{:S(2)}, u32[]{:S(2)}) %all-to-all-start.1) | async-done | bytes 131104 | tf_op jit(solution)/shard_map/all_to_all | solution.py:104
  102.1 0.2 reshape.627
  102.4 0.3 copy.94
  102.7 0.3 squeeze.69
  103.0 2.1 %fusion.35 = f32[8,8,256]{2,1,0:T(8,128)S(1)} fusion(bf16[8,64,8,8]{1,3,2,0:T(8,128)(2,1)S(1)} %squeeze.69, bf16[1,1,8,64,8,256]{5,4,3,2,1,0:T(8,128)(2,1)} %get-tuple-element.10), kind=kOutput, calls=%fused_computation.44 | convolution fusion | flops 16777216 | bytes 2228224 | tf_op jit(solution)/shard_map/mdlh,mdlu->umh/dot_general | solution.py:71
  105.1 0.3 copy.93
  105.4 0.3 squeeze.68
  105.7 2.1 %fusion.36 = f32[8,8,256]{2,1,0:T(8,128)S(1)} fusion(bf16[8,64,8,8]{1,3,2,0:T(8,128)(2,1)S(1)} %squeeze.68, bf16[1,1,8,64,8,256]{5,4,3,2,1,0:T(8,128)(2,1)} %get-tuple-element.10), kind=kOutput, calls=%fused_computation.45 | convolution fusion | flops 16777216 | bytes 2228224 | tf_op jit(solution)/shard_map/mdlh,mdlu->umh/dot_general | solution.py:71
  107.8 0.5 fusion.47
  108.3 0.5 fusion.48
  108.8 14.4 %all_gather.7 = bf16[4,2,8,2048]{3,2,1,0:T(8,128)(2,1)S(1)} all-gather(bf16[1,2,8,2048]{3,2,1,0:T(8,128)(2,1)S(1)} %pad_maximum_fusion.4), channel_id=1, replica_groups=mesh['groups'=2,'freq'=4,'tile'=4] {'freq'}, dimensions={0}, use_global_device_ids=true | all-gather | bytes 327680 | tf_op jit(solution)/shard_map/all_gather | solution.py:122
  123.3 6.0 %multiply_convert_fusion = bf16[2560,2048]{1,0:T(8,128)(2,1)} fusion(bf16[128,2048]{1,0:T(8,128)(2,1)S(1)} %bitcast.230, bf16[2560,8]{0,1:T(8,128)(2,1)S(1)} %convolution_convert_fusion, s32[128]{0:T(128)S(1)} %get-tuple-element.34, s32[2560]{0:T(1024)S(1)} %add_select_fusion.1, s32[128]{0:T(128)S(1)} %get-tuple-element.33), kind=kOutput, calls=%fused_computation | convolution fusion | flops 1358889984 | bytes 11062272 | tf_op jit(solution)/shard_map/dot_general | solution.py:126
  (52 shorter events, 1.5 us)
Async XLA Ops:
  6.5 37.7 %reduce-scatter.5.cloned.1.call-start = ((), (), s32[]{:S(2)}) async-start(), calls=%async_computation.5 | async-start | bytes 1310720 | tf_op jit(solution)/shard_map/reduce_scatter | solution.py:86
  14.2 7.3 %copy-start.6 = (s32[1,32,16]{1,2,0:T(8,128)S(1)}, s32[1,32,16]{1,2,0:T(8,128)}, u32[]{:S(2)}) copy-start(s32[1,32,16]{1,2,0:T(8,128)} %param.7) | copy-start | bytes 6148
  14.2 69.6 %reduce-scatter.3.cloned.1.call-start = ((), (), s32[]{:S(2)}) async-start(), calls=%async_computation.4 | async-start | bytes 1310720 | tf_op jit(solution)/shard_map/reduce_scatter | solution.py:86
  21.9 5.1 %copy-start.5 = (bf16[1,2,8,64,8,256]{5,4,3,2,1,0:T(8,128)(2,1)S(1)}, bf16[1,2,8,64,8,256]{5,4,3,2,1,0:T(8,128)(2,1)}, u32[]{:S(2)}) copy-start(bf16[1,2,8,64,8,256]{5,4,3,2,1,0:T(8,128)(2,1)} %param.6) | copy-start | bytes 12582916
  44.2 4.4 %copy-start.3 = (bf16[1,1,32,16,8,256]{5,4,3,2,1,0:T(8,128)(2,1)S(1)}, bf16[1,1,32,16,8,256]{5,4,3,2,1,0:T(8,128)(2,1)}, u32[]{:S(2)}) copy-start(bf16[1,1,32,16,8,256]{5,4,3,2,1,0:T(8,128)(2,1)} %get-tuple-element.12) | copy-start | bytes 6291460
  45.3 4.7 %copy-start.1 = (bf16[1,1,32,16,8,256]{5,4,3,2,1,0:T(8,128)(2,1)S(1)}, bf16[1,1,32,16,8,256]{5,4,3,2,1,0:T(8,128)(2,1)}, u32[]{:S(2)}) copy-start(bf16[1,1,32,16,8,256]{5,4,3,2,1,0:T(8,128)(2,1)} %get-tuple-element.11) | copy-start | bytes 6291460
  56.2 7.9 %all-to-all-start = ((bf16[4,2,8192]{2,1,0:T(2,128)(2,1)}), bf16[4,2,8192]{2,1,0:T(2,128)(2,1)S(1)}, u32[]{:S(2)}, u32[]{:S(2)}) async-start(bf16[4,2,8192]{2,1,0:T(2,128)(2,1)} %reshape.624), calls=%async_computation.2 | async-start | bytes 262144 | tf_op jit(solution)/shard_map/all_to_all | solution.py:104
  65.6 2.3 %copy-start = (bf16[1,1,8,64,8,256]{5,4,3,2,1,0:T(8,128)(2,1)S(1)}, bf16[1,1,8,64,8,256]{5,4,3,2,1,0:T(8,128)(2,1)}, u32[]{:S(2)}) copy-start(bf16[1,1,8,64,8,256]{5,4,3,2,1,0:T(8,128)(2,1)} %get-tuple-element.10) | copy-start | bytes 6291460
  83.8 4.4 %copy-start.4 = (bf16[1,1,32,16,8,256]{5,4,3,2,1,0:T(8,128)(2,1)S(1)}, bf16[1,1,32,16,8,256]{5,4,3,2,1,0:T(8,128)(2,1)}, u32[]{:S(2)}) copy-start(bf16[1,1,32,16,8,256]{5,4,3,2,1,0:T(8,128)(2,1)} %get-tuple-element.12) | copy-start | bytes 6291460
  85.0 4.7 %copy-start.2 = (bf16[1,1,32,16,8,256]{5,4,3,2,1,0:T(8,128)(2,1)S(1)}, bf16[1,1,32,16,8,256]{5,4,3,2,1,0:T(8,128)(2,1)}, u32[]{:S(2)}) copy-start(bf16[1,1,32,16,8,256]{5,4,3,2,1,0:T(8,128)(2,1)} %get-tuple-element.11) | copy-start | bytes 6291460
  94.2 7.9 %all-to-all-start.1 = ((bf16[4,2,8192]{2,1,0:T(2,128)(2,1)}), bf16[4,2,8192]{2,1,0:T(2,128)(2,1)S(1)}, u32[]{:S(2)}, u32[]{:S(2)}) async-start(bf16[4,2,8192]{2,1,0:T(2,128)(2,1)} %reshape.626), calls=%async_computation.3 | async-start | bytes 262144 | tf_op jit(solution)/shard_map/all_to_all | solution.py:104
Sparse Core Ops, SparseCore 0:
  14.3 29.8 reduce-scatter.4
  46.6 25.7 reduce-scatter.2
